TPU v7x, 32 devices: a whole 2x2x4 slice. The times are simulated.
32 devices in a mesh: dp: 8 (over y, x, core), tensor: 4 (over z).
Axes of the slice: x: 2, y: 2, z: 4, core: 2. Of those that a mesh axis runs over, the one named last changes fastest.
Arguments:
- glu_input: bfloat16 [16, 256, 3072], P('dp', 'tensor'), may hold values from -12 to 12
- depth_kernel: float32 [31, 1536], replicated, may hold values from -1 to 1
- norm_scale: float32 [1536], replicated, may hold values from 0.5 to 1.5
- norm_shift: float32 [1536], replicated, may hold values from -3 to 3
- proj_weight: bfloat16 [1536, 1536], P('tensor'), may hold values from -0.15625 to 0.15625
- out_grad: bfloat16 [16, 256, 1536], P('dp', 'tensor'), may hold values from -6 to 6
Outputs:
- conv_output: bfloat16 [16, 256, 1536], P('dp', 'tensor')
- input_grad: bfloat16 [16, 256, 3072], P('dp', 'tensor')
- weight_grad: float32 [1536, 1536], P('tensor')
- kernel_grad: float32 [31, 1536], replicated
- scale_grad: float32 [1536], replicated
- shift_grad: float32 [1536], replicated
All inputs are finite; a program needn't handle non-finite values.
Results may differ from a plain program's by a relative error of at most 0.0057.
Values may be sent and summed in bfloat16 or wider, within the bound.
No kernel may reach another device: no remote copies, remote signals or barrier semaphores. Data moves between devices by JAX's collectives and lax.ppermute only.
A program may use at most 128 MiB of HBM per device.

v0:
```python
import jax
import jax.numpy as jnp
from jax import lax
from jax.sharding import PartitionSpec as P

epsilon = 1e-05


def extended(array, sides, width):
    for axis, dim in sides:
        peers, length = (lax.axis_size(axis), array.shape[dim])
        up = [(i, (i + 1) % peers) for i in range(peers - 1)]
        down = [(j, i) for i, j in up]
        last = lax.slice_in_dim(array, length - width, length, axis=dim)
        leading = lax.slice_in_dim(array, 0, width, axis=dim)
        before = lax.ppermute(last, axis, up)
        after = lax.ppermute(leading, axis, down)
        array = jnp.concatenate([before, array, after], axis=dim)
    return array


def on_device(glu_input, depth_kernel, norm_scale, norm_shift, proj_weight, out_grad):
    width = proj_weight.shape[1]
    frames = glu_input.shape[1]
    taps = depth_kernel.shape[0]
    radius = (taps - 1) // 2
    everyone = glu_input.shape[0] * frames * lax.axis_size("dp") * lax.axis_size("tensor")
    values = glu_input[..., :width].astype(jnp.float32)
    gates = jax.nn.sigmoid(glu_input[..., width:].astype(jnp.float32))
    gated = (values * gates).astype(jnp.bfloat16)
    padded = extended(gated, (("tensor", 1),), radius)
    conv_out = jnp.zeros(gated.shape, jnp.float32)
    for offset in range(taps):
        conv_out = conv_out + depth_kernel[offset] * padded[:, offset : offset + frames, :]
    average = lax.psum(jnp.sum(conv_out, axis=(0, 1)), ("dp", "tensor")) / everyone
    centred = conv_out - average
    variance = lax.psum(jnp.sum(centred * centred, axis=(0, 1)), ("dp", "tensor")) / everyone
    inverse = lax.rsqrt(variance + epsilon)
    normed = centred * inverse
    affine = norm_scale * normed + norm_shift
    sig_affine = jax.nn.sigmoid(affine)
    activated = (affine * sig_affine).astype(jnp.bfloat16)
    full_weight = lax.all_gather(proj_weight, "tensor", axis=0, tiled=True)
    conv_output = jnp.einsum(
        "btc,cd->btd", activated, full_weight, preferred_element_type=jnp.float32
    ).astype(jnp.bfloat16)
    grad_act = jnp.einsum("btd,cd->btc", out_grad, full_weight, preferred_element_type=jnp.float32)
    grad_affine = grad_act * (sig_affine + affine * sig_affine * (1.0 - sig_affine))
    shift_grad, scale_grad = lax.psum(
        (jnp.sum(grad_affine, axis=(0, 1)), jnp.sum(grad_affine * normed, axis=(0, 1))),
        ("dp", "tensor"),
    )
    grad_conv = (
        norm_scale
        * inverse
        * (grad_affine - shift_grad / everyone - normed * scale_grad / everyone)
    ).astype(jnp.bfloat16)
    grad_pad = extended(grad_conv, (("tensor", 1),), radius)
    grad_gated = jnp.zeros(gated.shape, jnp.float32)
    for offset in range(taps):
        begin = 2 * radius - offset
        grad_gated = grad_gated + depth_kernel[offset] * grad_pad[:, begin : begin + frames, :]
    grad_wide = grad_conv.astype(jnp.float32)
    kernel_terms = jnp.stack(
        [
            jnp.sum(
                padded[:, offset : offset + frames, :].astype(jnp.float32) * grad_wide, axis=(0, 1)
            )
            for offset in range(taps)
        ]
    )
    kernel_grad = lax.psum(kernel_terms, ("dp", "tensor"))
    input_grad = jnp.concatenate(
        [grad_gated * gates, grad_gated * values * gates * (1.0 - gates)], axis=-1
    ).astype(jnp.bfloat16)
    partial_sum = jnp.einsum("btc,btd->cd", activated, out_grad, preferred_element_type=jnp.float32)
    received = lax.all_to_all(partial_sum[None], "tensor", split_axis=1, concat_axis=0, tiled=True)
    local_grad = jnp.sum(received, axis=0)
    weight_grad = lax.psum(local_grad, "dp")
    return (conv_output, input_grad, weight_grad, kernel_grad, scale_grad, shift_grad)


def solution(mesh):
    in_specs = (P("dp", "tensor", None), P(), P(), P(), P("tensor", None), P("dp", "tensor", None))
    out_specs = (P("dp", "tensor", None), P("dp", "tensor", None), P("tensor", None), P(), P(), P())
    return jax.shard_map(
        on_device, mesh=mesh, in_specs=in_specs, out_specs=out_specs, check_vma=False
    )
```

profile of v0, /device:TPU:0, one launch (start us, length us, event | category | flops | bytes accessed | tf_op | source)
XLA Modules:
  0.0 659.3 jit_solution(2058861156043940140)
XLA Ops:
  7.2 1.4 fusion.10
  8.6 4.9 collective-permute-start
  14.8 1.8 slice_reduce_fusion.30
  16.6 1.4 slice_reduce_fusion.29
  18.0 2.0 collective-permute-done.1
  20.0 3.8 fusion.154
  23.9 40.6 %psum.42 = f32[1536]{0:T(1024)S(1)} all-reduce(f32[1536]{0:T(1024)S(1)} %get-tuple-element.75), channel_id=1, replica_groups=mesh['dp'=8,'tensor'=4] {'dp','tensor'}, use_global_device_ids=true, to_apply=%region_1.0 | all-reduce | flops 1536 | bytes 12288 | tf_op jit(solution)/shard_map/psum | solution.py:35
  64.6 39.4 %psum.43 = f32[1536]{0:T(1024)S(1)} all-reduce(f32[1536]{0:T(1024)S(1)} %multiply_reduce_fusion.1), channel_id=1, replica_groups=mesh['dp'=8,'tensor'=4] {'dp','tensor'}, use_global_device_ids=true, to_apply=%region_3.0 | all-reduce | flops 1536 | bytes 12288 | tf_op jit(solution)/shard_map/psum | solution.py:37
  104.7 2.2 convolution_bitcast_fusion
  106.8 35.9 %copy.12 = f32[1,1536,1536]{2,0,1:T(1,128)} copy(f32[1,1536,1536]{2,1,0:T(8,128)S(1)} %convolution_bitcast_fusion) | data formatting | bytes 18874368 | tf_op jit(solution)/shard_map/broadcast_in_dim | solution.py:77
  142.8 5.9 all-to-all-start
  149.5 167.6 %all-gather.2.cloned.1.call-done = bf16[1536,1536]{1,0:T(8,128)(2,1)} async-done(((bf16[384,1536]{1,0:T(8,128)(2,1)}), bf16[1536,1536]{1,0:T(8,128)(2,1)}) %all-gather.2.cloned.1.call-update) | async-done | bytes 4718608 | tf_op jit(solution)/shard_map/all_gather | solution.py:43
  317.1 4.1 fusion.152
  321.2 128.5 %all-reduce = (f32[1536]{0:T(1024)S(1)}, f32[1536]{0:T(1024)S(1)}) all-reduce(f32[1536]{0:T(1024)S(1)} %get-tuple-element.38, f32[1536]{0:T(1024)S(1)} %get-tuple-element.37), channel_id=1, replica_groups=mesh['dp'=8,'tensor'=4] {'dp','tensor'}, use_global_device_ids=true, to_apply=%region_7.0 | all-reduce | flops 3072 | bytes 24576 | tf_op jit(solution)/shard_map/psum | solution.py:49
  449.7 1.5 fusion.90
  454.6 2.8 stack.127
  458.7 4.6 collective-permute-start.3
  463.3 4.0 fusion.7
  467.3 8.2 %copy.13 = f32[1,1536,1536]{2,1,0:T(8,128)} copy(f32[1,1536,1536]{2,0,1:T(1,128)} %all-to-all-done) | data formatting | bytes 18874368
  475.5 6.5 reduce_sum.328
  482.0 4.1 multiply_convert_fusion
  487.4 93.8 %all-reduce.6.cloned.1.call-done = f32[31,1536]{1,0:T(8,128)} async-done(((f32[31,1536]{1,0:T(8,128)}), f32[31,1536]{1,0:T(8,128)}) %all-reduce.6.cloned.1.call-update) | async-done | bytes 190480 | tf_op jit(solution)/shard_map/psum | solution.py:72
  581.2 67.7 %all-reduce.4.cloned.1.call-done = f32[384,1536]{1,0:T(8,128)} async-done(((f32[384,1536]{1,0:T(8,128)}), f32[384,1536]{1,0:T(8,128)}) %all-reduce.4.cloned.1.call-update) | async-done | bytes 2359312 | tf_op jit(solution)/shard_map/psum | solution.py:79
  648.9 3.2 copy.16
  (69 shorter events, 9.3 us)
Async XLA Ops:
  7.2 97.5 %copy-start = (bf16[2,64,1536]{2,1,0:T(8,128)(2,1)S(1)}, bf16[2,64,1536]{2,1,0:T(8,128)(2,1)}, u32[]{:S(2)}) copy-start(bf16[2,64,1536]{2,1,0:T(8,128)(2,1)} %param.11) | copy-start | bytes 1179652
  8.6 9.4 %collective-permute-start = (bf16[2,15,1536]{2,1,0:T(8,128)(2,1)S(1)}, bf16[2,15,1536]{2,1,0:T(8,128)(2,1)S(1)}, u32[]{:S(2)}, u32[]{:S(2)}) collective-permute-start(bf16[2,15,1536]{2,1,0:T(8,128)(2,1)S(1)} %get-tuple-element.79), channel_id=1, source_target_pairs={{0,1},{1,2},{2,3},{4,5},{5,6},{6,7},{8,9},{9,10},{10,11},{12,13},{... | collective-permute-start | bytes 276488 | tf_op jit(solution)/shard_map/ppermute | solution.py:16
  13.5 6.5 collective-permute-start.1
  142.8 174.4 %copy-start.3 = (f32[1536]{0:T(1024)S(1)}, f32[1536]{0:T(1024)}, u32[]{:S(2)}) copy-start(f32[1536]{0:T(1024)} %param.8) | copy-start | bytes 18436
  142.8 174.4 %copy-start.4 = (f32[1536]{0:T(1024)S(1)}, f32[1536]{0:T(1024)}, u32[]{:S(2)}) copy-start(f32[1536]{0:T(1024)} %param.9) | copy-start | bytes 18436
  142.8 324.5 %all-to-all-start = ((f32[1,1536,1536]{2,0,1:T(1,128)}), f32[1,1536,1536]{2,0,1:T(1,128)}, u32[]{:S(2)}, u32[]{:S(2)}) async-start(f32[1,1536,1536]{2,0,1:T(1,128)} %copy.12), calls=%async_computation | async-start | bytes 18874368 | tf_op jit(solution)/shard_map/all_to_all | solution.py:77
  148.7 168.4 %all-gather.2.cloned.1.call-start = ((), (), s32[]{:S(2)}) async-start(), calls=%async_computation.1 | async-start | bytes 5898240 | tf_op jit(solution)/shard_map/all_gather | solution.py:43
  149.4 431.7 %all-reduce.6.cloned.1.call-start = ((), (), s32[]{:S(2)}) async-start(), calls=%async_computation.3 | async-start | bytes 393216 | tf_op jit(solution)/shard_map/psum | solution.py:72
  449.7 17.6 %copy-start.5 = (f32[1536]{0:T(1024)}, f32[1536]{0:T(1024)S(1)}, u32[]{:S(2)}) copy-start(f32[1536]{0:T(1024)S(1)} %get-tuple-element.88) | copy-start | bytes 18436
  449.7 17.6 %copy-start.6 = (f32[1536]{0:T(1024)}, f32[1536]{0:T(1024)S(1)}, u32[]{:S(2)}) copy-start(f32[1536]{0:T(1024)S(1)} %get-tuple-element.89) | copy-start | bytes 18436
  457.3 191.6 %all-reduce.4.cloned.1.call-start = ((), (), s32[]{:S(2)}) async-start(), calls=%async_computation.2 | async-start | bytes 4718592 | tf_op jit(solution)/shard_map/psum | solution.py:79
  457.4 24.6 %collective-permute-start.2 = (bf16[2,15,1536]{2,1,0:T(8,128)(2,1)S(1)}, bf16[2,15,1536]{2,1,0:T(8,128)(2,1)S(1)}, u32[]{:S(2)}, u32[]{:S(2)}) collective-permute-start(bf16[2,15,1536]{2,1,0:T(8,128)(2,1)S(1)} %get-tuple-element.77), channel_id=1, source_target_pairs={{1,0},{2,1},{3,2},{5,4},{6,5},{7,6},{9,8},{10,9},{11,10},{13,12},{... | collective-permute-start | bytes 276488 | tf_op jit(solution)/shard_map/ppermute | solution.py:17
  458.7 23.3 %collective-permute-start.3 = (bf16[2,15,1536]{2,1,0:T(8,128)(2,1)S(1)}, bf16[2,15,1536]{2,1,0:T(8,128)(2,1)S(1)}, u32[]{:S(2)}, u32[]{:S(2)}) collective-permute-start(bf16[2,15,1536]{2,1,0:T(8,128)(2,1)S(1)} %get-tuple-element.78), channel_id=1, source_target_pairs={{0,1},{1,2},{2,3},{4,5},{5,6},{6,7},{8,9},{9,10},{10,11},{12,13},{... | collective-permute-start | bytes 276488 | tf_op jit(solution)/shard_map/ppermute | solution.py:16
  475.5 6.5 copy-start.1
  581.2 70.9 %copy-start.2 = (f32[31,1536]{1,0:T(8,128)S(1)}, f32[31,1536]{1,0:T(8,128)}, u32[]{:S(2)}) copy-start(f32[31,1536]{1,0:T(8,128)} %all-reduce.6.cloned.1.call-done) | copy-start | bytes 571396
Sparse Core Ops, SparseCore 0:
  151.1 165.9 all-gather.1
  457.5 123.6 all-reduce.5
  585.0 63.8 all-reduce.3
where the time goes:
time: 660 us; the launch traced here: 659 us
  waiting for transfers between devices  332 us (50%)
  blocking collectives  208 us (32%)
  local copies, waits for them, and re-layouts  54.2 us (8%)
  other arithmetic  22.2 us (3%)
  starting transfers between devices  18.1 us (3%)
  between operations  14.2 us (2%)
  matrix products  10.2 us (2%)
    all_gather x1, waiting for transfers between devices, on_device(): full_weight = lax.all_gather(proj_weight, 'tensor', axis=0, tiled=True)  168 us
    psum x1, blocking collectives, on_device(): lax.psum((jnp.sum(grad_affine, axis=(0, 1)), jnp.sum(grad_affine * normed...  129 us
    psum x1, waiting for transfers between devices, on_device(): kernel_grad = lax.psum(kernel_terms, ('dp', 'tensor'))  93.8 us
    psum x1, waiting for transfers between devices, on_device(): weight_grad = lax.psum(local_grad, 'dp')  67.7 us
    psum x1, blocking collectives, on_device(): lax.psum(jnp.sum(conv_out, axis=(0, 1)), ('dp', 'tensor')) / everyone  40.6 us
    psum x1, blocking collectives, on_device(): lax.psum(jnp.sum(centred * centred, axis=(0, 1)), ('dp', 'tensor'))  39.4 us
    broadcast_in_dim x1, local copies, waits for them, and re-layouts, on_device(): partial_sum[None]  35.9 us
  transfers between devices with their start and end apart: 8, of which 4 were waited for; matrix products, arithmetic and copies ran while one was open for 6% of the time, Pallas kernels for 0%

commit v1 on v0

--- a/solution.py
+++ b/solution.py
@@ -4,6 +4,11 @@
 from jax.sharding import PartitionSpec as P
 
 epsilon = 1e-05
+
+
+def gather_and_add(x, axis):
+    blocks = lax.all_gather(x, axis)
+    return jnp.sum(blocks, axis=0)
 
 
 def extended(array, sides, width):
@@ -34,7 +39,7 @@
         conv_out = conv_out + depth_kernel[offset] * padded[:, offset : offset + frames, :]
     average = lax.psum(jnp.sum(conv_out, axis=(0, 1)), ("dp", "tensor")) / everyone
     centred = conv_out - average
-    variance = lax.psum(jnp.sum(centred * centred, axis=(0, 1)), ("dp", "tensor")) / everyone
+    variance = gather_and_add(jnp.sum(centred * centred, axis=(0, 1)), ("dp", "tensor")) / everyone
     inverse = lax.rsqrt(variance + epsilon)
     normed = centred * inverse
     affine = norm_scale * normed + norm_shift

time: 660 us -> 682 us (1.033)
  blocking collectives: 208 us -> 236 us
    all_gather x0 -> x1, blocking collectives: none -> 67.5 us  [gather_and_add(): blocks = lax.all_gather(x, axis)]
    psum x1 -> x0, blocking collectives: 39.4 us -> none  [on_device(): lax.psum(jnp.sum(centred * centred, axis=(0, 1)), ('dp', 'tensor'))]
where the time goes in v1:
time: 682 us; the launch traced here: 681 us
  waiting for transfers between devices  328 us (48%)
  blocking collectives  236 us (35%)
  local copies, waits for them, and re-layouts  54.3 us (8%)
  other arithmetic  21.6 us (3%)
  starting transfers between devices  18 us (3%)
  between operations  14.2 us (2%)
  matrix products  9.46 us (1%)
    all_gather x1, waiting for transfers between devices, on_device(): full_weight = lax.all_gather(proj_weight, 'tensor', axis=0, tiled=True)  164 us
    psum x1, blocking collectives, on_device(): lax.psum((jnp.sum(grad_affine, axis=(0, 1)), jnp.sum(grad_affine * normed...  128 us
    psum x1, waiting for transfers between devices, on_device(): kernel_grad = lax.psum(kernel_terms, ('dp', 'tensor'))  93 us
    psum x1, waiting for transfers between devices, on_device(): weight_grad = lax.psum(local_grad, 'dp')  67.7 us
    all_gather x1, blocking collectives, gather_and_add(): blocks = lax.all_gather(x, axis)  67.5 us
    psum x1, blocking collectives, on_device(): lax.psum(jnp.sum(conv_out, axis=(0, 1)), ('dp', 'tensor')) / everyone  40.6 us
    broadcast_in_dim x1, local copies, waits for them, and re-layouts, on_device(): partial_sum[None]  35.9 us
  transfers between devices with their start and end apart: 8, of which 4 were waited for; matrix products, arithmetic and copies ran while one was open for 6% of the time, Pallas kernels for 0%

profile of v1, /device:TPU:0, one launch (start us, length us, event | category | flops | bytes accessed | tf_op | source)
XLA Modules:
  0.0 680.8 jit_solution(1181066866923348793)
XLA Ops:
  7.2 1.4 fusion.10
  8.6 4.9 collective-permute-start
  14.9 1.8 slice_reduce_fusion.30
  16.6 1.4 slice_reduce_fusion.29
  18.1 2.0 collective-permute-done.1
  20.1 3.8 fusion.154
  23.9 40.6 %psum.35 = f32[1536]{0:T(1024)S(1)} all-reduce(f32[1536]{0:T(1024)S(1)} %get-tuple-element.75), channel_id=1, replica_groups=mesh['dp'=8,'tensor'=4] {'dp','tensor'}, use_global_device_ids=true, to_apply=%region_1.0 | all-reduce | flops 1536 | bytes 12288 | tf_op jit(solution)/shard_map/psum | solution.py:40
  64.6 67.5 %all-gather.1 = f32[32,1,1536]{2,1,0:T(1,128)S(1)} all-gather(f32[1,1,1536]{2,1,0:T(1,128)S(1)} %reshape.58), channel_id=2, replica_groups=mesh['dp'=8,'tensor'=4] {'dp','tensor'}, dimensions={0}, use_global_device_ids=true | all-gather | bytes 202752 | tf_op jit(solution)/shard_map/all_gather | solution.py:10
  132.2 1.5 convolution_bitcast_fusion
  133.7 35.9 %copy.12 = f32[1,1536,1536]{2,0,1:T(1,128)} copy(f32[1,1536,1536]{2,1,0:T(8,128)S(1)} %convolution_bitcast_fusion) | data formatting | bytes 18874368 | tf_op jit(solution)/shard_map/broadcast_in_dim | solution.py:82
  169.6 5.8 all-to-all-start
  176.2 164.1 %all-gather.4.cloned.1.call-done = bf16[1536,1536]{1,0:T(8,128)(2,1)} async-done(((bf16[384,1536]{1,0:T(8,128)(2,1)}), bf16[1536,1536]{1,0:T(8,128)(2,1)}) %all-gather.4.cloned.1.call-update) | async-done | bytes 4718608 | tf_op jit(solution)/shard_map/all_gather | solution.py:48
  340.3 4.1 fusion.152
  344.4 127.7 %all-reduce = (f32[1536]{0:T(1024)S(1)}, f32[1536]{0:T(1024)S(1)}) all-reduce(f32[1536]{0:T(1024)S(1)} %get-tuple-element.38, f32[1536]{0:T(1024)S(1)} %get-tuple-element.37), channel_id=1, replica_groups=mesh['dp'=8,'tensor'=4] {'dp','tensor'}, use_global_device_ids=true, to_apply=%region_7.0 | all-reduce | flops 3072 | bytes 24576 | tf_op jit(solution)/shard_map/psum | solution.py:54
  472.0 1.5 fusion.90
  476.9 2.8 stack.127
  481.0 4.6 collective-permute-start.3
  485.6 4.0 fusion.7
  489.6 8.2 %copy.13 = f32[1,1536,1536]{2,1,0:T(8,128)} copy(f32[1,1536,1536]{2,0,1:T(1,128)} %all-to-all-done) | data formatting | bytes 18874368
  497.8 6.5 reduce_sum.338
  504.3 4.1 multiply_convert_fusion
  509.7 93.0 %all-reduce.6.cloned.1.call-done = f32[31,1536]{1,0:T(8,128)} async-done(((f32[31,1536]{1,0:T(8,128)}), f32[31,1536]{1,0:T(8,128)}) %all-reduce.6.cloned.1.call-update) | async-done | bytes 190480 | tf_op jit(solution)/shard_map/psum | solution.py:77
  602.6 67.7 %all-reduce.4.cloned.1.call-done = f32[384,1536]{1,0:T(8,128)} async-done(((f32[384,1536]{1,0:T(8,128)}), f32[384,1536]{1,0:T(8,128)}) %all-reduce.4.cloned.1.call-update) | async-done | bytes 2359312 | tf_op jit(solution)/shard_map/psum | solution.py:84
  670.3 3.2 copy.16
  (71 shorter events, 8.7 us)
Async XLA Ops:
  7.2 125.1 %copy-start = (bf16[2,64,1536]{2,1,0:T(8,128)(2,1)S(1)}, bf16[2,64,1536]{2,1,0:T(8,128)(2,1)}, u32[]{:S(2)}) copy-start(bf16[2,64,1536]{2,1,0:T(8,128)(2,1)} %param.11) | copy-start | bytes 1179652
  7.2 125.0 %copy-start.3 = (f32[1536]{0:T(1024)S(1)}, f32[1536]{0:T(1024)}, u32[]{:S(2)}) copy-start(f32[1536]{0:T(1024)} %param.8) | copy-start | bytes 18436
  7.2 125.0 %copy-start.4 = (f32[1536]{0:T(1024)S(1)}, f32[1536]{0:T(1024)}, u32[]{:S(2)}) copy-start(f32[1536]{0:T(1024)} %param.9) | copy-start | bytes 18436
  8.6 9.4 %collective-permute-start = (bf16[2,15,1536]{2,1,0:T(8,128)(2,1)S(1)}, bf16[2,15,1536]{2,1,0:T(8,128)(2,1)S(1)}, u32[]{:S(2)}, u32[]{:S(2)}) collective-permute-start(bf16[2,15,1536]{2,1,0:T(8,128)(2,1)S(1)} %get-tuple-element.79), channel_id=1, source_target_pairs={{0,1},{1,2},{2,3},{4,5},{5,6},{6,7},{8,9},{9,10},{10,11},{12,13},{... | collective-permute-start | bytes 276488 | tf_op jit(solution)/shard_map/ppermute | solution.py:21
  13.6 6.5 collective-permute-start.1
  169.6 320.0 %all-to-all-start = ((f32[1,1536,1536]{2,0,1:T(1,128)}), f32[1,1536,1536]{2,0,1:T(1,128)}, u32[]{:S(2)}, u32[]{:S(2)}) async-start(f32[1,1536,1536]{2,0,1:T(1,128)} %copy.12), calls=%async_computation | async-start | bytes 18874368 | tf_op jit(solution)/shard_map/all_to_all | solution.py:82
  175.4 164.9 %all-gather.4.cloned.1.call-start = ((), (), s32[]{:S(2)}) async-start(), calls=%async_computation.1 | async-start | bytes 5898240 | tf_op jit(solution)/shard_map/all_gather | solution.py:48
  176.2 426.5 %all-reduce.6.cloned.1.call-start = ((), (), s32[]{:S(2)}) async-start(), calls=%async_computation.3 | async-start | bytes 393216 | tf_op jit(solution)/shard_map/psum | solution.py:77
  472.0 17.5 %copy-start.5 = (f32[1536]{0:T(1024)}, f32[1536]{0:T(1024)S(1)}, u32[]{:S(2)}) copy-start(f32[1536]{0:T(1024)S(1)} %get-tuple-element.88) | copy-start | bytes 18436
  472.0 17.5 %copy-start.6 = (f32[1536]{0:T(1024)}, f32[1536]{0:T(1024)S(1)}, u32[]{:S(2)}) copy-start(f32[1536]{0:T(1024)S(1)} %get-tuple-element.89) | copy-start | bytes 18436
  479.7 190.7 %all-reduce.4.cloned.1.call-start = ((), (), s32[]{:S(2)}) async-start(), calls=%async_computation.2 | async-start | bytes 4718592 | tf_op jit(solution)/shard_map/psum | solution.py:84
  479.7 24.6 %collective-permute-start.2 = (bf16[2,15,1536]{2,1,0:T(8,128)(2,1)S(1)}, bf16[2,15,1536]{2,1,0:T(8,128)(2,1)S(1)}, u32[]{:S(2)}, u32[]{:S(2)}) collective-permute-start(bf16[2,15,1536]{2,1,0:T(8,128)(2,1)S(1)} %get-tuple-element.77), channel_id=1, source_target_pairs={{1,0},{2,1},{3,2},{5,4},{6,5},{7,6},{9,8},{10,9},{11,10},{13,12},{... | collective-permute-start | bytes 276488 | tf_op jit(solution)/shard_map/ppermute | solution.py:22
  481.0 23.3 %collective-permute-start.3 = (bf16[2,15,1536]{2,1,0:T(8,128)(2,1)S(1)}, bf16[2,15,1536]{2,1,0:T(8,128)(2,1)S(1)}, u32[]{:S(2)}, u32[]{:S(2)}) collective-permute-start(bf16[2,15,1536]{2,1,0:T(8,128)(2,1)S(1)} %get-tuple-element.78), channel_id=1, source_target_pairs={{0,1},{1,2},{2,3},{4,5},{5,6},{6,7},{8,9},{9,10},{10,11},{12,13},{... | collective-permute-start | bytes 276488 | tf_op jit(solution)/shard_map/ppermute | solution.py:21
  497.8 6.5 copy-start.1
  602.6 70.9 %copy-start.2 = (f32[31,1536]{1,0:T(8,128)S(1)}, f32[31,1536]{1,0:T(8,128)}, u32[]{:S(2)}) copy-start(f32[31,1536]{1,0:T(8,128)} %all-reduce.6.cloned.1.call-done) | copy-start | bytes 571396
Sparse Core Ops, SparseCore 0:
  177.8 162.4 all-gather.3
  479.8 122.8 all-reduce.5
  606.5 63.8 all-reduce.3
